TPU v7x, 32 devices: a whole 2x2x4 slice. The times are simulated.
32 devices in a mesh: groups: 2 (over y), tm: 16 (over z, x, core).
Axes of the slice: x: 2, y: 2, z: 4, core: 2. Of those that a mesh axis runs over, the one named last changes fastest.
Arguments:
- ref_traj: float32 [8, 1024, 256], P('groups', 'tm'), parts along dimension 0, may hold values from -6 to 6
- cost_weights: float32 [8, 1024, 256], P('groups', 'tm'), parts along dimension 0, may hold values from 0.1 to 10
- x_init: float32 [8, 256], P('groups'), parts along dimension 0, may hold values from -6 to 6
- decay: float32 [256], replicated, as said below
- coupling: float32 [3, 64, 64], replicated, may hold values from -0.00018310547 to 0.00018310547
- links: int32 [3, 2], replicated, may hold values from 0 to 3, as said below
- input_map: float32 [256, 64], replicated, may hold values from -0.0007324219 to 0.0007324219
- ff_gain: float32 [64, 256], replicated, may hold values from -0.01171875 to 0.01171875
- lengths: int32 [8, 4], P('groups'), parts along dimension 0, may hold values from 1 to 512, 1024 in all within a row
Outputs:
- states: float32 [8, 1024, 256], P('groups', 'tm'), parts along dimension 0
- weight_grad: float32 [8, 1024, 256], P('groups', 'tm'), parts along dimension 0
- cost: float32 [8], P('groups'), parts along dimension 0
There are 2 independent parts, one for each index of `groups`. A program takes and returns all parts, laid end to end along the dimension named above; an argument that names none is the same for every part. Nothing has to cross between parts.
Inputs may be any that keep to these rules, and one draw needn't show every extreme that they name: `links`: each pair names two different blocks, the row before the column, and no pair twice. The lengths of a scenario sum to 1024, and the longest is exactly 512. `decay`: every entry lies strictly between 0 and 1.
All inputs are finite; a program needn't handle non-finite values.
Results may differ from a plain program's by a relative error of at most 0.0003.
Values sent between devices are 32-bit elements; how exact they have to be, the bound alone decides.
No kernel may reach another device: no remote copies, remote signals or barrier semaphores. Data moves between devices by JAX's collectives and lax.ppermute only.
A program may use at most 64 MiB of HBM per device.

v0:
```python
import jax
import jax.numpy as jnp
from jax import lax
from jax.sharding import PartitionSpec as P


def build_dynamics(decay, coupling, links):
    size = decay.shape[0]
    width = coupling.shape[1]
    lanes = jnp.arange(size, dtype=jnp.int32)
    offsets = jnp.arange(width, dtype=jnp.int32)
    row_hot = (lanes[None, :, None] == links[:, 0:1, None] * width + offsets[None, None, :]).astype(
        jnp.float32
    )
    col_hot = (lanes[None, :, None] == links[:, 1:2, None] * width + offsets[None, None, :]).astype(
        jnp.float32
    )
    placed = jnp.einsum(
        "lia,lab,ljb->ij", row_hot, coupling, col_hot, precision=lax.Precision.HIGHEST
    )
    return jnp.diag(decay) + placed


def row_times(values, matrix):
    width = values.shape[-1]
    flat = jnp.dot(values.reshape(-1, width), matrix, precision=lax.Precision.HIGHEST)
    return flat.reshape(values.shape)


def run_chain(inputs, frame_starts, powers, backward, local_levels, device_levels):
    scen_count, seg_steps, width = inputs.shape
    devices = lax.axis_size("tm")
    device = lax.axis_index("tm")
    if backward:
        driven = inputs[:, ::-1]
        frame_device = devices - 1 - device
    else:
        driven = inputs
        frame_device = device
    positions = frame_device * seg_steps + jnp.arange(seg_steps, dtype=jnp.int32)
    cut_here = jnp.any(positions[None, :, None] == frame_starts[:, None, :], axis=-1)
    values = driven
    flags = 1.0 - cut_here.astype(jnp.float32)
    for level in range(local_levels):
        stride = 2**level
        prior_values = jnp.pad(values[:, : seg_steps - stride], ((0, 0), (stride, 0), (0, 0)))
        prior_flags = jnp.pad(
            flags[:, : seg_steps - stride], ((0, 0), (stride, 0)), constant_values=1.0
        )
        values = values + flags[:, :, None] * row_times(prior_values, powers[level])
        flags = flags * prior_flags
    last_value = values[:, -1]
    last_flag = flags[:, -1]
    all_values, all_flags = (
        lax.all_gather(last_value[None], "tm", axis=0, tiled=True),
        lax.all_gather(last_flag[None], "tm", axis=0, tiled=True),
    )
    if backward:
        all_values = all_values[::-1]
        all_flags = all_flags[::-1]
    roll_by = devices - frame_device
    all_values = jnp.roll(all_values, roll_by, axis=0)
    all_flags = jnp.roll(all_flags, roll_by, axis=0)
    keep = (jnp.arange(devices, dtype=jnp.int32) >= roll_by).astype(jnp.float32)
    all_values = all_values * keep[:, None, None]
    all_flags = all_flags * keep[:, None] + (1.0 - keep[:, None])
    for level in range(device_levels):
        half = all_values.shape[0] // 2
        paired_values = all_values.reshape(half, 2, scen_count, width)
        paired_flags = all_flags.reshape(half, 2, scen_count)
        moved = row_times(paired_values[:, 0], powers[local_levels + level])
        all_values = paired_flags[:, 1, :, None] * moved + paired_values[:, 1]
        all_flags = paired_flags[:, 0] * paired_flags[:, 1]
    entering = all_values[0]
    table = row_times(entering[:, None, :], powers[0])
    for level in range(local_levels):
        table = jnp.concatenate([table, row_times(table, powers[level])], axis=1)
    result = values + flags[:, :, None] * table
    if backward:
        result = result[:, ::-1]
    return result


def per_device(ref_traj, cost_weights, x_init, decay, coupling, links, input_map, ff_gain, lengths):
    scen_count, seg_steps, width = ref_traj.shape
    devices = lax.axis_size("tm")
    device = lax.axis_index("tm")
    total = seg_steps * devices
    high = lax.Precision.HIGHEST
    dynamics = build_dynamics(decay, coupling, links)
    local_levels = seg_steps.bit_length() - 1
    device_levels = (devices - 1).bit_length()
    power_count = local_levels + max(device_levels, 1)
    squares = [dynamics]
    for level in range(power_count - 1):
        squares.append(jnp.dot(squares[-1], squares[-1], precision=high))
    forward_powers = [matrix.T for matrix in squares]
    ends_incl = jnp.cumsum(lengths, axis=1)
    starts = ends_incl - lengths
    mirrored = total - ends_incl
    value_term = run_chain(
        cost_weights * ref_traj, mirrored, squares, True, local_levels, device_levels
    )
    controls = jnp.einsum("stn,cn->stc", value_term, ff_gain, precision=high)
    forcing = -jnp.einsum("stc,nc->stn", controls, input_map, precision=high)
    positions = device * seg_steps + jnp.arange(seg_steps, dtype=jnp.int32)
    start_flag = jnp.any(positions[None, :, None] == starts[:, None, :], axis=-1).astype(
        jnp.float32
    )
    init_image = jnp.dot(x_init, dynamics.T, precision=high)
    driven = forcing + start_flag[:, :, None] * init_image[:, None, :]
    states = run_chain(driven, starts, forward_powers, False, local_levels, device_levels)
    offset = states - ref_traj
    local_cost = jnp.sum(cost_weights * offset * offset, axis=(1, 2)) * (0.5 / total)
    cost = lax.psum(local_cost, "tm")
    adjoint = run_chain(cost_weights * offset, mirrored, squares, True, local_levels, device_levels)
    pulled = jnp.einsum("stn,nc->stc", adjoint, input_map, precision=high)
    source = -jnp.einsum("stc,cn->stn", pulled, ff_gain, precision=high)
    value_adjoint = run_chain(source, starts, forward_powers, False, local_levels, device_levels)
    weight_grad = 0.5 * offset * offset + ref_traj * value_adjoint
    return (states, weight_grad, cost)


def solution(mesh):
    placed = (
        P("groups", "tm", None),
        P("groups", "tm", None),
        P("groups", None),
        P(),
        P(),
        P(),
        P(),
        P(),
        P("groups", None),
    )
    return jax.shard_map(
        per_device,
        mesh=mesh,
        in_specs=placed,
        out_specs=(P("groups", "tm", None), P("groups", "tm", None), P("groups")),
        check_vma=False,
    )
```

profile of v0, /device:TPU:0, one launch (start us, length us, event | category | flops | bytes accessed | tf_op | source)
XLA Modules:
  0.0 228.4 jit_solution(11940536303902532036)
XLA Ops:
  0.7 0.6 copy-done.79
  1.4 0.6 dynamic-slice
  2.7 0.7 copy-done.78
  3.3 0.7 copy-done.66
  5.6 0.5 copy-done.47
  6.1 0.6 convert_element_type.84
  6.9 0.5 copy-done.30
  7.5 0.5 copy-done.24
  8.1 0.5 copy-done.21
  8.6 0.5 copy-done.18
  9.9 34.9 %all-reduce.38 = (f32[64]{0:T(128)S(1)}, f32[64]{0:T(128)S(1)}) all-reduce(f32[64]{0:T(128)S(1)} %dynamic-update-slice, f32[64]{0:T(128)S(1)} %dynamic-update-slice.1), channel_id=2, replica_groups=mesh['groups'=2,'tm'=16] {'tm'}, use_global_device_ids=true, to_apply=%add.36 | all-reduce | flops 128 | bytes 1024
  45.9 0.6 slice_multiply_fusion.2
  46.5 0.6 slice_multiply_fusion.4
  47.0 0.5 slice_bitcast_fusion.24
  47.5 0.7 copy.317
  49.6 0.9 convolution_bitcast_fusion.2
  54.0 0.5 copy-done.1
  54.7 0.8 rev.22
  55.4 0.8 slice.317
  56.4 1.3 fusion.23
  59.8 17.5 %all-gather.1 = f32[64,1,256]{2,1,0:T(1,128)S(1)} all-gather(f32[4,1,256]{2,1,0:T(1,128)S(1)} %slice.420), channel_id=3, replica_groups=mesh['groups'=2,'tm'=16] {'tm'}, dimensions={0}, use_global_device_ids=true | all-gather | bytes 69632 | tf_op jit(solution)/shard_map/all_gather | solution.py:55
  80.4 0.6 copy-done.6
  81.0 0.9 fusion.68
  81.9 2.5 %concatenate.103 = f32[4,64,256]{2,1,0:T(8,128)S(1)} concatenate(f32[4,1,256]{2,1,0:T(1,128)} %copy-done.14, f32[4,1,256]{2,1,0:T(1,128)} %copy-done.16, f32[4,2,256]{2,1,0:T(2,128)} %copy-done.12, f32[4,4,256]{2,1,0:T(4,128)S(1)} %fusion.104, f32[4,8,256]{2,1,0:T(8,128)S(1)} %fusion.92, f32[4,16,256]{2,1,0:T(8,128)} %copy-done.6, f32[4,32,256]{2,1,0:T(8,128)} %fusion.68), dimensions={1} | concatenate | bytes 524288 | tf_op jit(solution)/shard_map/concatenate | solution.py:77
  84.4 1.5 multiply_add_fusion.2
  85.9 1.0 rev.25
  90.2 0.6 copy-done.25
  91.3 0.6 copy-done.22
  92.4 0.6 copy-done.19
  93.5 19.2 %all-gather.3 = f32[64,1,256]{2,1,0:T(1,128)S(1)} all-gather(f32[4,1,256]{2,1,0:T(1,128)S(1)} %slice.441), channel_id=5, replica_groups=mesh['groups'=2,'tm'=16] {'tm'}, dimensions={0}, use_global_device_ids=true | all-gather | bytes 69632 | tf_op jit(solution)/shard_map/all_gather | solution.py:55
  112.9 0.5 copy-done.68
  113.6 0.7 copy-done.52
  114.7 0.7 copy-done.56
  115.7 0.6 copy-done.61
  119.4 1.1 fusion.65
  120.5 3.5 %concatenate.109 = f32[4,64,256]{2,1,0:T(8,128)} concatenate(f32[4,1,256]{2,1,0:T(1,128)S(1)} %reshape.528, f32[4,1,256]{2,1,0:T(1,128)S(1)} %reshape.529, f32[4,2,256]{2,1,0:T(2,128)S(1)} %copy.331, f32[4,4,256]{2,1,0:T(4,128)S(1)} %fusion.101, f32[4,8,256]{2,1,0:T(8,128)S(1)} %fusion.89, f32[4,16,256]{2,1,0:T(8,128)S(1)} %fusion.77, f32[4,32,256]{2,1,0:T(8,128)} %fusion.65), dimensions={1} | concatenate | bytes 524288 | tf_op jit(solution)/shard_map/concatenate | solution.py:77
  124.0 1.9 multiply_reduce_fusion
  125.9 30.3 %psum.7 = f32[4]{0:T(128)} all-reduce(f32[4]{0:T(128)S(1)} %broadcast_multiply_fusion), channel_id=1, replica_groups=mesh['groups'=2,'tm'=16] {'tm'}, use_global_device_ids=true, to_apply=%region_4.7 | all-reduce | flops 4 | bytes 32 | tf_op jit(solution)/shard_map/psum | solution.py:115
  156.3 0.8 rev.26
  157.0 0.8 slice.378
  158.0 1.3 fusion.11
  160.5 0.6 copy-done.38
  161.5 0.7 copy-done.36
  162.5 0.7 copy-done.34
  163.6 17.5 %all-gather.4 = f32[64,1,256]{2,1,0:T(1,128)S(1)} all-gather(f32[4,1,256]{2,1,0:T(1,128)S(1)} %slice.456), channel_id=6, replica_groups=mesh['groups'=2,'tm'=16] {'tm'}, dimensions={0}, use_global_device_ids=true | all-gather | bytes 69632 | tf_op jit(solution)/shard_map/all_gather | solution.py:55
  181.3 0.6 copy-done.71
  182.1 0.7 copy-done.55
  183.1 0.7 copy-done.59
  184.0 0.7 copy-done.64
  187.2 0.6 copy-done.7
  187.8 0.9 fusion.62
  188.7 2.5 %concatenate.115 = f32[4,64,256]{2,1,0:T(8,128)S(1)} concatenate(f32[4,1,256]{2,1,0:T(1,128)} %copy-done.15, f32[4,1,256]{2,1,0:T(1,128)} %copy-done.17, f32[4,2,256]{2,1,0:T(2,128)} %copy-done.13, f32[4,4,256]{2,1,0:T(4,128)S(1)} %fusion.98, f32[4,8,256]{2,1,0:T(8,128)S(1)} %fusion.86, f32[4,16,256]{2,1,0:T(8,128)} %copy-done.7, f32[4,32,256]{2,1,0:T(8,128)} %fusion.62), dimensions={1} | concatenate | bytes 524288 | tf_op jit(solution)/shard_map/concatenate | solution.py:77
  191.2 1.5 multiply_add_fusion
  192.7 1.0 rev.28
  197.0 0.6 copy-done.26
  198.1 0.6 copy-done.23
  199.2 0.6 copy-done.20
  200.3 19.2 %all-gather.5 = f32[64,1,256]{2,1,0:T(1,128)S(1)} all-gather(f32[4,1,256]{2,1,0:T(1,128)S(1)} %slice.471), channel_id=7, replica_groups=mesh['groups'=2,'tm'=16] {'tm'}, dimensions={0}, use_global_device_ids=true | all-gather | bytes 69632 | tf_op jit(solution)/shard_map/all_gather | solution.py:55
  219.7 0.5 copy-done.69
  220.4 0.7 copy-done.53
  221.5 0.7 copy-done.57
  222.5 0.6 copy-done.62
  226.7 0.9 copy-done.3
  227.6 0.8 fusion.46
  (328 shorter events, 36.9 us)
Async XLA Ops:
  0.6 47.6 %copy-start = (f32[3,64,64]{2,1,0:T(8,128)S(1)}, f32[3,64,64]{2,1,0:T(8,128)}, u32[]{:S(2)}) copy-start(f32[3,64,64]{2,1,0:T(8,128)} %param.17) | copy-start | bytes 147460
  0.7 0.7 copy-start.79
  2.6 74.9 %copy-start.70 = (f32[16]{0:T(128)}, f32[16]{0:T(128)S(1)}, u32[]{:S(2)}) copy-start(f32[16]{0:T(128)S(1)} %compare_convert_fusion.1) | copy-start | bytes 196
  2.6 43.0 %copy-start.67 = (f32[16]{0:T(128)}, f32[16]{0:T(128)S(1)}, u32[]{:S(2)}) copy-start(f32[16]{0:T(128)S(1)} %compare_convert_fusion) | copy-start | bytes 196
  2.7 0.7 copy-start.78
  3.3 0.7 copy-start.66
  4.3 51.9 %copy-start.50 = (f32[4,64]{1,0:T(4,128)}, f32[4,64]{1,0:T(4,128)S(1)}, u32[]{:S(2)}) copy-start(f32[4,64]{1,0:T(4,128)S(1)} %convert_subtract_fusion) | copy-start | bytes 3076
  4.4 53.3 %copy-start.41 = (f32[4,64]{1,0:T(4,128)}, f32[4,64]{1,0:T(4,128)S(1)}, u32[]{:S(2)}) copy-start(f32[4,64]{1,0:T(4,128)S(1)} %pad_multiply_fusion.11) | copy-start | bytes 3076
  4.5 53.7 %copy-start.39 = (f32[4,64]{1,0:T(4,128)}, f32[4,64]{1,0:T(4,128)S(1)}, u32[]{:S(2)}) copy-start(f32[4,64]{1,0:T(4,128)S(1)} %pad_multiply_fusion.10) | copy-start | bytes 3076
  4.6 54.0 %copy-start.37 = (f32[4,64]{1,0:T(4,128)}, f32[4,64]{1,0:T(4,128)S(1)}, u32[]{:S(2)}) copy-start(f32[4,64]{1,0:T(4,128)S(1)} %pad_multiply_fusion.9) | copy-start | bytes 3076
  4.6 54.4 %copy-start.35 = (f32[4,64]{1,0:T(4,128)}, f32[4,64]{1,0:T(4,128)S(1)}, u32[]{:S(2)}) copy-start(f32[4,64]{1,0:T(4,128)S(1)} %pad_multiply_fusion.8) | copy-start | bytes 3076
  4.7 54.7 %copy-start.33 = (f32[4,64]{1,0:T(4,128)}, f32[4,64]{1,0:T(4,128)S(1)}, u32[]{:S(2)}) copy-start(f32[4,64]{1,0:T(4,128)S(1)} %pad_multiply_fusion.7) | copy-start | bytes 3076
  45.3 32.7 %copy-start.58 = (f32[4,1,4]{2,1,0:T(1,128)}, f32[4,1,4]{2,1,0:T(1,128)S(1)}, u32[]{:S(2)}) copy-start(f32[4,1,4]{2,1,0:T(1,128)S(1)} %get-tuple-element.34) | copy-start | bytes 196
  45.3 32.9 %copy-start.63 = (f32[2,1,4]{2,1,0:T(1,128)}, f32[2,1,4]{2,1,0:T(1,128)S(1)}, u32[]{:S(2)}) copy-start(f32[2,1,4]{2,1,0:T(1,128)S(1)} %get-tuple-element.38) | copy-start | bytes 100
  45.3 33.1 %copy-start.75 = (f32[4]{0:T(128)}, f32[4]{0:T(128)S(1)}, u32[]{:S(2)}) copy-start(f32[4]{0:T(128)S(1)} %slice_bitcast_fusion.25) | copy-start | bytes 52
  45.4 32.2 %copy-start.54 = (f32[8,1,4]{0,2,1:T(4,128)}, f32[8,1,4]{0,2,1:T(4,128)S(1)}, u32[]{:S(2)}) copy-start(f32[8,1,4]{0,2,1:T(4,128)S(1)} %copy.299) | copy-start | bytes 388
  48.2 0.7 copy-start.77
  48.9 0.7 copy-start.72
  53.6 1.0 copy-start.1
  53.6 1.0 copy-start.2
  55.4 0.9 copy-start.5
  79.0 1.4 copy-start.14
  79.2 1.1 copy-start.16
  79.5 0.8 copy-start.12
  85.9 1.0 copy-start.10
  86.9 0.8 copy-start.8
  86.9 0.8 copy-start.60
  87.0 0.8 copy-start.65
  87.8 0.7 copy-start.48
  88.4 0.7 copy-start.28
  89.1 0.7 copy-start.31
  90.2 0.7 copy-start.25
  91.3 0.7 copy-start.22
  92.4 0.7 copy-start.19
  113.6 0.7 copy-start.52
  114.7 0.7 copy-start.56
  115.7 0.7 copy-start.61
  120.5 3.5 %copy-start.44 = (f32[4,64]{1,0:T(4,128)S(1)}, f32[4,64]{1,0:T(4,128)}, u32[]{:S(2)}) copy-start(f32[4,64]{1,0:T(4,128)} %copy-done.43) | copy-start | bytes 3076
  157.0 0.9 copy-start.4
  157.0 1.0 copy-start.51
  158.0 1.4 copy-start.42
  159.4 0.7 copy-start.40
  161.4 0.7 copy-start.36
  162.5 0.7 copy-start.34
  181.3 0.7 copy-start.71
  182.1 0.7 copy-start.55
  183.1 0.7 copy-start.59
  184.0 0.7 copy-start.64
  185.7 1.4 copy-start.15
  186.0 1.1 copy-start.17
  186.3 0.8 copy-start.13
  192.7 1.0 copy-start.9
  193.7 0.8 copy-start.11
  194.6 0.7 copy-start.49
  195.2 0.7 copy-start.29
  195.9 0.7 copy-start.32
  197.0 0.7 copy-start.26
  198.1 0.7 copy-start.23
  199.2 0.7 copy-start.20
  220.3 0.7 copy-start.53
  221.4 0.7 copy-start.57
  222.4 0.7 copy-start.62
  226.6 1.0 copy-start.3
  226.6 0.9 copy-start.45
  (16 other events, 9.5 us)
where the time goes:
time: 230 us; the launch traced here: 228 us
  blocking collectives  139 us (60%)
  local copies, waits for them, and re-layouts  44.1 us (19%)
  matrix products  32.4 us (14%)
  other arithmetic  10.2 us (4%)
  between operations  3.01 us (1%)
    all_gather x4, blocking collectives, run_chain(): lax.all_gather(last_value[None], 'tm', axis=0, tiled=True)  73.5 us
    unnamed x1, blocking collectives  34.9 us
    psum x1, blocking collectives, per_device(): cost = lax.psum(local_cost, 'tm')  30.3 us
    unnamed x165, local copies, waits for them, and re-layouts  27.1 us
    dot_general x68, matrix products, row_times(): jnp.dot(values.reshape(-1, width), matrix, precision=lax.Precision.HIGHEST)  25.8 us
    concatenate x12, local copies, waits for them, and re-layouts, run_chain(): table = jnp.concatenate([table, row_times(table, powers[level])], axis=1)  8.84 us

commit v1 on v0

--- a/solution.py
+++ b/solution.py
@@ -2,6 +2,19 @@
 import jax.numpy as jnp
 from jax import lax
 from jax.sharding import PartitionSpec as P
+
+
+def gather_around(value, axis, dim):
+    devices, index, rows = (lax.axis_size(axis), lax.axis_index(axis), value.shape[dim])
+    upward = [(i, (i + 1) % devices) for i in range(devices)]
+    out = jnp.zeros((*value.shape[:dim], devices * rows, *value.shape[dim + 1 :]), value.dtype)
+    current = value
+    for step in range(devices):
+        source = (index - step) % devices
+        out = lax.dynamic_update_slice_in_dim(out, current, source * rows, axis=dim)
+        if step < devices - 1:
+            current = lax.ppermute(current, axis, upward)
+    return out
 
 
 def build_dynamics(decay, coupling, links):
@@ -52,7 +65,7 @@
     last_value = values[:, -1]
     last_flag = flags[:, -1]
     all_values, all_flags = (
-        lax.all_gather(last_value[None], "tm", axis=0, tiled=True),
+        gather_around(last_value[None], "tm", 0),
         lax.all_gather(last_flag[None], "tm", axis=0, tiled=True),
     )
     if backward:

time: 230 us -> 479 us (2.08)
  waiting for transfers between devices: 0 us -> 332 us
  blocking collectives: 139 us -> 69.1 us
  local copies, waits for them, and re-layouts: 44.1 us -> 33.5 us
    ppermute x0 -> x60, waiting for transfers between devices: none -> 332 us  [gather_around(): current = lax.ppermute(current, axis, upward)]
    all_gather x4 -> x0, blocking collectives: 73.5 us -> none  [run_chain(): lax.all_gather(last_value[None], 'tm', axis=0, tiled=True)]
    unnamed x165 -> x129, local copies, waits for them, and re-layouts: 27.1 us -> 20.7 us
  transfers between devices with their start and end apart: 0 -> 60, of which waited for: 0 -> 58; matrix products, arithmetic and copies ran while one was open for 0% -> 2% of each run, Pallas kernels for 0% -> 0%
where the time goes in v1:
time: 479 us; the launch traced here: 478 us
  waiting for transfers between devices  332 us (69%)
  blocking collectives  69.1 us (14%)
  local copies, waits for them, and re-layouts  33.5 us (7%)
  matrix products  30.9 us (6%)
  other arithmetic  9.27 us (2%)
    ppermute x60, waiting for transfers between devices, gather_around(): current = lax.ppermute(current, axis, upward)  332 us
    unnamed x1, blocking collectives  34.7 us
    psum x1, blocking collectives, per_device(): cost = lax.psum(local_cost, 'tm')  34.4 us
    dot_general x68, matrix products, row_times(): jnp.dot(values.reshape(-1, width), matrix, precision=lax.Precision.HIGHEST)  24.4 us
    unnamed x129, local copies, waits for them, and re-layouts  20.7 us
  transfers between devices with their start and end apart: 60, of which 58 were waited for; matrix products, arithmetic and copies ran while one was open for 2% of the time, Pallas kernels for 0%

profile of v1, /device:TPU:0, one launch (start us, length us, event | category | flops | bytes accessed | tf_op | source)
XLA Modules:
  0.0 478.2 jit_solution(10078735134394712403)
XLA Ops:
  17.1 34.7 %all-reduce.38 = (f32[64]{0:T(128)S(1)}, f32[64]{0:T(128)S(1)}) all-reduce(f32[64]{0:T(128)S(1)} %dynamic-update-slice, f32[64]{0:T(128)S(1)} %dynamic-update-slice.1), channel_id=2, replica_groups=mesh['groups'=2,'tm'=16] {'tm'}, use_global_device_ids=true, to_apply=%add.36 | all-reduce | flops 128 | bytes 1024
  58.3 5.7 %collective-permute-done.1 = f32[1,4,256]{2,0,1:T(1,128)S(1)} collective-permute-done((f32[1,4,256]{2,0,1:T(1,128)S(1)}, f32[1,4,256]{2,0,1:T(1,128)S(1)}, u32[]{:S(2)}, u32[]{:S(2)}) %collective-permute-start.1) | collective-permute-done | bytes 4128 | tf_op jit(solution)/shard_map/ppermute | solution.py:16
  64.0 5.7 %collective-permute-done.2 = f32[1,4,256]{2,0,1:T(1,128)S(1)} collective-permute-done((f32[1,4,256]{2,0,1:T(1,128)S(1)}, f32[1,4,256]{2,0,1:T(1,128)S(1)}, u32[]{:S(2)}, u32[]{:S(2)}) %collective-permute-start.2) | collective-permute-done | bytes 4128 | tf_op jit(solution)/shard_map/ppermute | solution.py:16
  69.7 5.7 %collective-permute-done.3 = f32[1,4,256]{2,0,1:T(1,128)S(1)} collective-permute-done((f32[1,4,256]{2,0,1:T(1,128)S(1)}, f32[1,4,256]{2,0,1:T(1,128)S(1)}, u32[]{:S(2)}, u32[]{:S(2)}) %collective-permute-start.3) | collective-permute-done | bytes 4128 | tf_op jit(solution)/shard_map/ppermute | solution.py:16
  75.5 5.7 %collective-permute-done.4 = f32[1,4,256]{2,0,1:T(1,128)S(1)} collective-permute-done((f32[1,4,256]{2,0,1:T(1,128)S(1)}, f32[1,4,256]{2,0,1:T(1,128)S(1)}, u32[]{:S(2)}, u32[]{:S(2)}) %collective-permute-start.4) | collective-permute-done | bytes 4128 | tf_op jit(solution)/shard_map/ppermute | solution.py:16
  81.2 5.7 %collective-permute-done.5 = f32[1,4,256]{2,0,1:T(1,128)S(1)} collective-permute-done((f32[1,4,256]{2,0,1:T(1,128)S(1)}, f32[1,4,256]{2,0,1:T(1,128)S(1)}, u32[]{:S(2)}, u32[]{:S(2)}) %collective-permute-start.5) | collective-permute-done | bytes 4128 | tf_op jit(solution)/shard_map/ppermute | solution.py:16
  86.9 5.7 %collective-permute-done.6 = f32[1,4,256]{2,0,1:T(1,128)S(1)} collective-permute-done((f32[1,4,256]{2,0,1:T(1,128)S(1)}, f32[1,4,256]{2,0,1:T(1,128)S(1)}, u32[]{:S(2)}, u32[]{:S(2)}) %collective-permute-start.6) | collective-permute-done | bytes 4128 | tf_op jit(solution)/shard_map/ppermute | solution.py:16
  92.7 5.7 %collective-permute-done.7 = f32[1,4,256]{2,0,1:T(1,128)S(1)} collective-permute-done((f32[1,4,256]{2,0,1:T(1,128)S(1)}, f32[1,4,256]{2,0,1:T(1,128)S(1)}, u32[]{:S(2)}, u32[]{:S(2)}) %collective-permute-start.7) | collective-permute-done | bytes 4128 | tf_op jit(solution)/shard_map/ppermute | solution.py:16
  98.4 5.7 %collective-permute-done.8 = f32[1,4,256]{2,0,1:T(1,128)S(1)} collective-permute-done((f32[1,4,256]{2,0,1:T(1,128)S(1)}, f32[1,4,256]{2,0,1:T(1,128)S(1)}, u32[]{:S(2)}, u32[]{:S(2)}) %collective-permute-start.8) | collective-permute-done | bytes 4128 | tf_op jit(solution)/shard_map/ppermute | solution.py:16
  104.1 5.7 %collective-permute-done.9 = f32[1,4,256]{2,0,1:T(1,128)S(1)} collective-permute-done((f32[1,4,256]{2,0,1:T(1,128)S(1)}, f32[1,4,256]{2,0,1:T(1,128)S(1)}, u32[]{:S(2)}, u32[]{:S(2)}) %collective-permute-start.9) | collective-permute-done | bytes 4128 | tf_op jit(solution)/shard_map/ppermute | solution.py:16
  109.9 5.7 %collective-permute-done.10 = f32[1,4,256]{2,0,1:T(1,128)S(1)} collective-permute-done((f32[1,4,256]{2,0,1:T(1,128)S(1)}, f32[1,4,256]{2,0,1:T(1,128)S(1)}, u32[]{:S(2)}, u32[]{:S(2)}) %collective-permute-start.10) | collective-permute-done | bytes 4128 | tf_op jit(solution)/shard_map/ppermute | solution.py:16
  115.6 5.7 %collective-permute-done.11 = f32[1,4,256]{2,0,1:T(1,128)S(1)} collective-permute-done((f32[1,4,256]{2,0,1:T(1,128)S(1)}, f32[1,4,256]{2,0,1:T(1,128)S(1)}, u32[]{:S(2)}, u32[]{:S(2)}) %collective-permute-start.11) | collective-permute-done | bytes 4128 | tf_op jit(solution)/shard_map/ppermute | solution.py:16
  121.3 5.7 %collective-permute-done.12 = f32[1,4,256]{2,0,1:T(1,128)S(1)} collective-permute-done((f32[1,4,256]{2,0,1:T(1,128)S(1)}, f32[1,4,256]{2,0,1:T(1,128)S(1)}, u32[]{:S(2)}, u32[]{:S(2)}) %collective-permute-start.12) | collective-permute-done | bytes 4128 | tf_op jit(solution)/shard_map/ppermute | solution.py:16
  127.0 5.7 %collective-permute-done.13 = f32[1,4,256]{2,0,1:T(1,128)S(1)} collective-permute-done((f32[1,4,256]{2,0,1:T(1,128)S(1)}, f32[1,4,256]{2,0,1:T(1,128)S(1)}, u32[]{:S(2)}, u32[]{:S(2)}) %collective-permute-start.13) | collective-permute-done | bytes 4128 | tf_op jit(solution)/shard_map/ppermute | solution.py:16
  132.8 5.7 %collective-permute-done.14 = f32[1,4,256]{2,0,1:T(1,128)S(1)} collective-permute-done((f32[1,4,256]{2,0,1:T(1,128)S(1)}, f32[1,4,256]{2,0,1:T(1,128)S(1)}, u32[]{:S(2)}, u32[]{:S(2)}) %collective-permute-start.14) | collective-permute-done | bytes 4128 | tf_op jit(solution)/shard_map/ppermute | solution.py:16
  146.9 5.7 %collective-permute-done.15 = f32[1,4,256]{2,0,1:T(1,128)S(1)} collective-permute-done((f32[1,4,256]{2,0,1:T(1,128)S(1)}, f32[1,4,256]{2,0,1:T(1,128)S(1)}, u32[]{:S(2)}, u32[]{:S(2)}) %collective-permute-start.15) | collective-permute-done | bytes 4128 | tf_op jit(solution)/shard_map/ppermute | solution.py:16
  152.6 5.7 %collective-permute-done.16 = f32[1,4,256]{2,0,1:T(1,128)S(1)} collective-permute-done((f32[1,4,256]{2,0,1:T(1,128)S(1)}, f32[1,4,256]{2,0,1:T(1,128)S(1)}, u32[]{:S(2)}, u32[]{:S(2)}) %collective-permute-start.16) | collective-permute-done | bytes 4128 | tf_op jit(solution)/shard_map/ppermute | solution.py:16
  158.3 5.7 %collective-permute-done.17 = f32[1,4,256]{2,0,1:T(1,128)S(1)} collective-permute-done((f32[1,4,256]{2,0,1:T(1,128)S(1)}, f32[1,4,256]{2,0,1:T(1,128)S(1)}, u32[]{:S(2)}, u32[]{:S(2)}) %collective-permute-start.17) | collective-permute-done | bytes 4128 | tf_op jit(solution)/shard_map/ppermute | solution.py:16
  164.1 5.7 %collective-permute-done.18 = f32[1,4,256]{2,0,1:T(1,128)S(1)} collective-permute-done((f32[1,4,256]{2,0,1:T(1,128)S(1)}, f32[1,4,256]{2,0,1:T(1,128)S(1)}, u32[]{:S(2)}, u32[]{:S(2)}) %collective-permute-start.18) | collective-permute-done | bytes 4128 | tf_op jit(solution)/shard_map/ppermute | solution.py:16
  169.8 5.7 %collective-permute-done.19 = f32[1,4,256]{2,0,1:T(1,128)S(1)} collective-permute-done((f32[1,4,256]{2,0,1:T(1,128)S(1)}, f32[1,4,256]{2,0,1:T(1,128)S(1)}, u32[]{:S(2)}, u32[]{:S(2)}) %collective-permute-start.19) | collective-permute-done | bytes 4128 | tf_op jit(solution)/shard_map/ppermute | solution.py:16
  175.5 5.7 %collective-permute-done.20 = f32[1,4,256]{2,0,1:T(1,128)S(1)} collective-permute-done((f32[1,4,256]{2,0,1:T(1,128)S(1)}, f32[1,4,256]{2,0,1:T(1,128)S(1)}, u32[]{:S(2)}, u32[]{:S(2)}) %collective-permute-start.20) | collective-permute-done | bytes 4128 | tf_op jit(solution)/shard_map/ppermute | solution.py:16
  181.2 5.7 %collective-permute-done.21 = f32[1,4,256]{2,0,1:T(1,128)S(1)} collective-permute-done((f32[1,4,256]{2,0,1:T(1,128)S(1)}, f32[1,4,256]{2,0,1:T(1,128)S(1)}, u32[]{:S(2)}, u32[]{:S(2)}) %collective-permute-start.21) | collective-permute-done | bytes 4128 | tf_op jit(solution)/shard_map/ppermute | solution.py:16
  187.0 5.7 %collective-permute-done.22 = f32[1,4,256]{2,0,1:T(1,128)S(1)} collective-permute-done((f32[1,4,256]{2,0,1:T(1,128)S(1)}, f32[1,4,256]{2,0,1:T(1,128)S(1)}, u32[]{:S(2)}, u32[]{:S(2)}) %collective-permute-start.22) | collective-permute-done | bytes 4128 | tf_op jit(solution)/shard_map/ppermute | solution.py:16
  192.7 5.7 %collective-permute-done.23 = f32[1,4,256]{2,0,1:T(1,128)S(1)} collective-permute-done((f32[1,4,256]{2,0,1:T(1,128)S(1)}, f32[1,4,256]{2,0,1:T(1,128)S(1)}, u32[]{:S(2)}, u32[]{:S(2)}) %collective-permute-start.23) | collective-permute-done | bytes 4128 | tf_op jit(solution)/shard_map/ppermute | solution.py:16
  198.4 5.7 %collective-permute-done.24 = f32[1,4,256]{2,0,1:T(1,128)S(1)} collective-permute-done((f32[1,4,256]{2,0,1:T(1,128)S(1)}, f32[1,4,256]{2,0,1:T(1,128)S(1)}, u32[]{:S(2)}, u32[]{:S(2)}) %collective-permute-start.24) | collective-permute-done | bytes 4128 | tf_op jit(solution)/shard_map/ppermute | solution.py:16
  204.2 5.7 %collective-permute-done.25 = f32[1,4,256]{2,0,1:T(1,128)S(1)} collective-permute-done((f32[1,4,256]{2,0,1:T(1,128)S(1)}, f32[1,4,256]{2,0,1:T(1,128)S(1)}, u32[]{:S(2)}, u32[]{:S(2)}) %collective-permute-start.25) | collective-permute-done | bytes 4128 | tf_op jit(solution)/shard_map/ppermute | solution.py:16
  209.9 5.7 %collective-permute-done.26 = f32[1,4,256]{2,0,1:T(1,128)S(1)} collective-permute-done((f32[1,4,256]{2,0,1:T(1,128)S(1)}, f32[1,4,256]{2,0,1:T(1,128)S(1)}, u32[]{:S(2)}, u32[]{:S(2)}) %collective-permute-start.26) | collective-permute-done | bytes 4128 | tf_op jit(solution)/shard_map/ppermute | solution.py:16
  215.6 5.7 %collective-permute-done.27 = f32[1,4,256]{2,0,1:T(1,128)S(1)} collective-permute-done((f32[1,4,256]{2,0,1:T(1,128)S(1)}, f32[1,4,256]{2,0,1:T(1,128)S(1)}, u32[]{:S(2)}, u32[]{:S(2)}) %collective-permute-start.27) | collective-permute-done | bytes 4128 | tf_op jit(solution)/shard_map/ppermute | solution.py:16
  221.4 5.7 %collective-permute-done.28 = f32[1,4,256]{2,0,1:T(1,128)S(1)} collective-permute-done((f32[1,4,256]{2,0,1:T(1,128)S(1)}, f32[1,4,256]{2,0,1:T(1,128)S(1)}, u32[]{:S(2)}, u32[]{:S(2)}) %collective-permute-start.28) | collective-permute-done | bytes 4128 | tf_op jit(solution)/shard_map/ppermute | solution.py:16
  227.1 5.7 %collective-permute-done.29 = f32[1,4,256]{2,0,1:T(1,128)S(1)} collective-permute-done((f32[1,4,256]{2,0,1:T(1,128)S(1)}, f32[1,4,256]{2,0,1:T(1,128)S(1)}, u32[]{:S(2)}, u32[]{:S(2)}) %collective-permute-start.29) | collective-permute-done | bytes 4128 | tf_op jit(solution)/shard_map/ppermute | solution.py:16
  239.8 3.5 concatenate.109
  243.3 1.9 multiply_reduce_fusion
  250.5 34.4 %psum.7 = f32[4]{0:T(128)} all-reduce(f32[4]{0:T(128)S(1)} %broadcast_multiply_fusion), channel_id=1, replica_groups=mesh['groups'=2,'tm'=16] {'tm'}, use_global_device_ids=true, to_apply=%region_4.7 | all-reduce | flops 4 | bytes 32 | tf_op jit(solution)/shard_map/psum | solution.py:128
  284.9 5.7 %collective-permute-done.31 = f32[1,4,256]{2,0,1:T(1,128)S(1)} collective-permute-done((f32[1,4,256]{2,0,1:T(1,128)S(1)}, f32[1,4,256]{2,0,1:T(1,128)S(1)}, u32[]{:S(2)}, u32[]{:S(2)}) %collective-permute-start.31) | collective-permute-done | bytes 4128 | tf_op jit(solution)/shard_map/ppermute | solution.py:16
  290.7 5.7 %collective-permute-done.32 = f32[1,4,256]{2,0,1:T(1,128)S(1)} collective-permute-done((f32[1,4,256]{2,0,1:T(1,128)S(1)}, f32[1,4,256]{2,0,1:T(1,128)S(1)}, u32[]{:S(2)}, u32[]{:S(2)}) %collective-permute-start.32) | collective-permute-done | bytes 4128 | tf_op jit(solution)/shard_map/ppermute | solution.py:16
  296.4 5.7 %collective-permute-done.33 = f32[1,4,256]{2,0,1:T(1,128)S(1)} collective-permute-done((f32[1,4,256]{2,0,1:T(1,128)S(1)}, f32[1,4,256]{2,0,1:T(1,128)S(1)}, u32[]{:S(2)}, u32[]{:S(2)}) %collective-permute-start.33) | collective-permute-done | bytes 4128 | tf_op jit(solution)/shard_map/ppermute | solution.py:16
  302.1 5.7 %collective-permute-done.34 = f32[1,4,256]{2,0,1:T(1,128)S(1)} collective-permute-done((f32[1,4,256]{2,0,1:T(1,128)S(1)}, f32[1,4,256]{2,0,1:T(1,128)S(1)}, u32[]{:S(2)}, u32[]{:S(2)}) %collective-permute-start.34) | collective-permute-done | bytes 4128 | tf_op jit(solution)/shard_map/ppermute | solution.py:16
  307.8 5.7 %collective-permute-done.35 = f32[1,4,256]{2,0,1:T(1,128)S(1)} collective-permute-done((f32[1,4,256]{2,0,1:T(1,128)S(1)}, f32[1,4,256]{2,0,1:T(1,128)S(1)}, u32[]{:S(2)}, u32[]{:S(2)}) %collective-permute-start.35) | collective-permute-done | bytes 4128 | tf_op jit(solution)/shard_map/ppermute | solution.py:16
  313.6 5.7 %collective-permute-done.36 = f32[1,4,256]{2,0,1:T(1,128)S(1)} collective-permute-done((f32[1,4,256]{2,0,1:T(1,128)S(1)}, f32[1,4,256]{2,0,1:T(1,128)S(1)}, u32[]{:S(2)}, u32[]{:S(2)}) %collective-permute-start.36) | collective-permute-done | bytes 4128 | tf_op jit(solution)/shard_map/ppermute | solution.py:16
  319.3 5.7 %collective-permute-done.37 = f32[1,4,256]{2,0,1:T(1,128)S(1)} collective-permute-done((f32[1,4,256]{2,0,1:T(1,128)S(1)}, f32[1,4,256]{2,0,1:T(1,128)S(1)}, u32[]{:S(2)}, u32[]{:S(2)}) %collective-permute-start.37) | collective-permute-done | bytes 4128 | tf_op jit(solution)/shard_map/ppermute | solution.py:16
  325.0 5.7 %collective-permute-done.38 = f32[1,4,256]{2,0,1:T(1,128)S(1)} collective-permute-done((f32[1,4,256]{2,0,1:T(1,128)S(1)}, f32[1,4,256]{2,0,1:T(1,128)S(1)}, u32[]{:S(2)}, u32[]{:S(2)}) %collective-permute-start.38) | collective-permute-done | bytes 4128 | tf_op jit(solution)/shard_map/ppermute | solution.py:16
  330.8 5.7 %collective-permute-done.39 = f32[1,4,256]{2,0,1:T(1,128)S(1)} collective-permute-done((f32[1,4,256]{2,0,1:T(1,128)S(1)}, f32[1,4,256]{2,0,1:T(1,128)S(1)}, u32[]{:S(2)}, u32[]{:S(2)}) %collective-permute-start.39) | collective-permute-done | bytes 4128 | tf_op jit(solution)/shard_map/ppermute | solution.py:16
  336.5 5.7 %collective-permute-done.40 = f32[1,4,256]{2,0,1:T(1,128)S(1)} collective-permute-done((f32[1,4,256]{2,0,1:T(1,128)S(1)}, f32[1,4,256]{2,0,1:T(1,128)S(1)}, u32[]{:S(2)}, u32[]{:S(2)}) %collective-permute-start.40) | collective-permute-done | bytes 4128 | tf_op jit(solution)/shard_map/ppermute | solution.py:16
  342.2 5.7 %collective-permute-done.41 = f32[1,4,256]{2,0,1:T(1,128)S(1)} collective-permute-done((f32[1,4,256]{2,0,1:T(1,128)S(1)}, f32[1,4,256]{2,0,1:T(1,128)S(1)}, u32[]{:S(2)}, u32[]{:S(2)}) %collective-permute-start.41) | collective-permute-done | bytes 4128 | tf_op jit(solution)/shard_map/ppermute | solution.py:16
  348.0 5.7 %collective-permute-done.42 = f32[1,4,256]{2,0,1:T(1,128)S(1)} collective-permute-done((f32[1,4,256]{2,0,1:T(1,128)S(1)}, f32[1,4,256]{2,0,1:T(1,128)S(1)}, u32[]{:S(2)}, u32[]{:S(2)}) %collective-permute-start.42) | collective-permute-done | bytes 4128 | tf_op jit(solution)/shard_map/ppermute | solution.py:16
  353.7 5.7 %collective-permute-done.43 = f32[1,4,256]{2,0,1:T(1,128)S(1)} collective-permute-done((f32[1,4,256]{2,0,1:T(1,128)S(1)}, f32[1,4,256]{2,0,1:T(1,128)S(1)}, u32[]{:S(2)}, u32[]{:S(2)}) %collective-permute-start.43) | collective-permute-done | bytes 4128 | tf_op jit(solution)/shard_map/ppermute | solution.py:16
  359.4 5.7 %collective-permute-done.44 = f32[1,4,256]{2,0,1:T(1,128)S(1)} collective-permute-done((f32[1,4,256]{2,0,1:T(1,128)S(1)}, f32[1,4,256]{2,0,1:T(1,128)S(1)}, u32[]{:S(2)}, u32[]{:S(2)}) %collective-permute-start.44) | collective-permute-done | bytes 4128 | tf_op jit(solution)/shard_map/ppermute | solution.py:16
  372.5 2.5 concatenate.115
  375.0 1.5 multiply_add_fusion
  384.2 5.7 %collective-permute-done.45 = f32[1,4,256]{2,0,1:T(1,128)S(1)} collective-permute-done((f32[1,4,256]{2,0,1:T(1,128)S(1)}, f32[1,4,256]{2,0,1:T(1,128)S(1)}, u32[]{:S(2)}, u32[]{:S(2)}) %collective-permute-start.45) | collective-permute-done | bytes 4128 | tf_op jit(solution)/shard_map/ppermute | solution.py:16
  389.9 5.7 %collective-permute-done.46 = f32[1,4,256]{2,0,1:T(1,128)S(1)} collective-permute-done((f32[1,4,256]{2,0,1:T(1,128)S(1)}, f32[1,4,256]{2,0,1:T(1,128)S(1)}, u32[]{:S(2)}, u32[]{:S(2)}) %collective-permute-start.46) | collective-permute-done | bytes 4128 | tf_op jit(solution)/shard_map/ppermute | solution.py:16
  395.6 5.7 %collective-permute-done.47 = f32[1,4,256]{2,0,1:T(1,128)S(1)} collective-permute-done((f32[1,4,256]{2,0,1:T(1,128)S(1)}, f32[1,4,256]{2,0,1:T(1,128)S(1)}, u32[]{:S(2)}, u32[]{:S(2)}) %collective-permute-start.47) | collective-permute-done | bytes 4128 | tf_op jit(solution)/shard_map/ppermute | solution.py:16
  401.3 5.7 %collective-permute-done.48 = f32[1,4,256]{2,0,1:T(1,128)S(1)} collective-permute-done((f32[1,4,256]{2,0,1:T(1,128)S(1)}, f32[1,4,256]{2,0,1:T(1,128)S(1)}, u32[]{:S(2)}, u32[]{:S(2)}) %collective-permute-start.48) | collective-permute-done | bytes 4128 | tf_op jit(solution)/shard_map/ppermute | solution.py:16
  407.1 5.7 %collective-permute-done.49 = f32[1,4,256]{2,0,1:T(1,128)S(1)} collective-permute-done((f32[1,4,256]{2,0,1:T(1,128)S(1)}, f32[1,4,256]{2,0,1:T(1,128)S(1)}, u32[]{:S(2)}, u32[]{:S(2)}) %collective-permute-start.49) | collective-permute-done | bytes 4128 | tf_op jit(solution)/shard_map/ppermute | solution.py:16
  412.8 5.7 %collective-permute-done.50 = f32[1,4,256]{2,0,1:T(1,128)S(1)} collective-permute-done((f32[1,4,256]{2,0,1:T(1,128)S(1)}, f32[1,4,256]{2,0,1:T(1,128)S(1)}, u32[]{:S(2)}, u32[]{:S(2)}) %collective-permute-start.50) | collective-permute-done | bytes 4128 | tf_op jit(solution)/shard_map/ppermute | solution.py:16
  418.5 5.7 %collective-permute-done.51 = f32[1,4,256]{2,0,1:T(1,128)S(1)} collective-permute-done((f32[1,4,256]{2,0,1:T(1,128)S(1)}, f32[1,4,256]{2,0,1:T(1,128)S(1)}, u32[]{:S(2)}, u32[]{:S(2)}) %collective-permute-start.51) | collective-permute-done | bytes 4128 | tf_op jit(solution)/shard_map/ppermute | solution.py:16
  424.3 5.7 %collective-permute-done.52 = f32[1,4,256]{2,0,1:T(1,128)S(1)} collective-permute-done((f32[1,4,256]{2,0,1:T(1,128)S(1)}, f32[1,4,256]{2,0,1:T(1,128)S(1)}, u32[]{:S(2)}, u32[]{:S(2)}) %collective-permute-start.52) | collective-permute-done | bytes 4128 | tf_op jit(solution)/shard_map/ppermute | solution.py:16
  430.0 5.7 %collective-permute-done.53 = f32[1,4,256]{2,0,1:T(1,128)S(1)} collective-permute-done((f32[1,4,256]{2,0,1:T(1,128)S(1)}, f32[1,4,256]{2,0,1:T(1,128)S(1)}, u32[]{:S(2)}, u32[]{:S(2)}) %collective-permute-start.53) | collective-permute-done | bytes 4128 | tf_op jit(solution)/shard_map/ppermute | solution.py:16
  435.7 5.7 %collective-permute-done.54 = f32[1,4,256]{2,0,1:T(1,128)S(1)} collective-permute-done((f32[1,4,256]{2,0,1:T(1,128)S(1)}, f32[1,4,256]{2,0,1:T(1,128)S(1)}, u32[]{:S(2)}, u32[]{:S(2)}) %collective-permute-start.54) | collective-permute-done | bytes 4128 | tf_op jit(solution)/shard_map/ppermute | solution.py:16
  441.4 5.7 %collective-permute-done.55 = f32[1,4,256]{2,0,1:T(1,128)S(1)} collective-permute-done((f32[1,4,256]{2,0,1:T(1,128)S(1)}, f32[1,4,256]{2,0,1:T(1,128)S(1)}, u32[]{:S(2)}, u32[]{:S(2)}) %collective-permute-start.55) | collective-permute-done | bytes 4128 | tf_op jit(solution)/shard_map/ppermute | solution.py:16
  447.2 5.7 %collective-permute-done.56 = f32[1,4,256]{2,0,1:T(1,128)S(1)} collective-permute-done((f32[1,4,256]{2,0,1:T(1,128)S(1)}, f32[1,4,256]{2,0,1:T(1,128)S(1)}, u32[]{:S(2)}, u32[]{:S(2)}) %collective-permute-start.56) | collective-permute-done | bytes 4128 | tf_op jit(solution)/shard_map/ppermute | solution.py:16
  452.9 5.7 %collective-permute-done.57 = f32[1,4,256]{2,0,1:T(1,128)S(1)} collective-permute-done((f32[1,4,256]{2,0,1:T(1,128)S(1)}, f32[1,4,256]{2,0,1:T(1,128)S(1)}, u32[]{:S(2)}, u32[]{:S(2)}) %collective-permute-start.57) | collective-permute-done | bytes 4128 | tf_op jit(solution)/shard_map/ppermute | solution.py:16
  458.6 5.7 %collective-permute-done.58 = f32[1,4,256]{2,0,1:T(1,128)S(1)} collective-permute-done((f32[1,4,256]{2,0,1:T(1,128)S(1)}, f32[1,4,256]{2,0,1:T(1,128)S(1)}, u32[]{:S(2)}, u32[]{:S(2)}) %collective-permute-start.58) | collective-permute-done | bytes 4128 | tf_op jit(solution)/shard_map/ppermute | solution.py:16
  464.4 5.7 %collective-permute-done.59 = f32[1,4,256]{2,0,1:T(1,128)S(1)} collective-permute-done((f32[1,4,256]{2,0,1:T(1,128)S(1)}, f32[1,4,256]{2,0,1:T(1,128)S(1)}, u32[]{:S(2)}, u32[]{:S(2)}) %collective-permute-start.59) | collective-permute-done | bytes 4128 | tf_op jit(solution)/shard_map/ppermute | solution.py:16
  (470 shorter events, 65.1 us)
Async XLA Ops:
  12.6 45.7 %collective-permute-start = (f32[1,4,256]{2,0,1:T(1,128)S(1)}, f32[1,4,256]{2,0,1:T(1,128)S(1)}, u32[]{:S(2)}, u32[]{:S(2)}) collective-permute-start(f32[1,4,256]{2,0,1:T(1,128)S(1)} %slice_bitcast_fusion.27), channel_id=1, source_target_pairs={{0,1},{1,2},{2,3},{3,4},{4,5},{5,6},{6,7},{7,8},{8,9},{9,10},{10,1... | collective-permute-start | bytes 12296 | tf_op jit(solution)/shard_map/ppermute | solution.py:16
  14.5 130.9 %copy-start.20 = (f32[4,64]{1,0:T(4,128)}, f32[4,64]{1,0:T(4,128)S(1)}, u32[]{:S(2)}) copy-start(f32[4,64]{1,0:T(4,128)S(1)} %pad_multiply_fusion.3) | copy-start | bytes 3076
  14.6 131.3 %copy-start.18 = (f32[4,64]{1,0:T(4,128)}, f32[4,64]{1,0:T(4,128)S(1)}, u32[]{:S(2)}) copy-start(f32[4,64]{1,0:T(4,128)S(1)} %pad_multiply_fusion.2) | copy-start | bytes 3076
  14.7 131.7 %copy-start.16 = (f32[4,64]{1,0:T(4,128)}, f32[4,64]{1,0:T(4,128)S(1)}, u32[]{:S(2)}) copy-start(f32[4,64]{1,0:T(4,128)S(1)} %pad_multiply_fusion.1) | copy-start | bytes 3076
  14.8 228.5 %copy-start.26 = (f32[4,64]{1,0:T(4,128)}, f32[4,64]{1,0:T(4,128)S(1)}, u32[]{:S(2)}) copy-start(f32[4,64]{1,0:T(4,128)S(1)} %pad_multiply_fusion) | copy-start | bytes 3076
  58.3 5.7 %collective-permute-start.1 = (f32[1,4,256]{2,0,1:T(1,128)S(1)}, f32[1,4,256]{2,0,1:T(1,128)S(1)}, u32[]{:S(2)}, u32[]{:S(2)}) collective-permute-start(f32[1,4,256]{2,0,1:T(1,128)S(1)} %collective-permute-done), channel_id=1, source_target_pairs={{0,1},{1,2},{2,3},{3,4},{4,5},{5,6},{6,7},{7,8},{8,9},{9,10},{10,1... | collective-permute-start | bytes 12296 | tf_op jit(solution)/shard_map/ppermute | solution.py:16
  64.0 5.7 %collective-permute-start.2 = (f32[1,4,256]{2,0,1:T(1,128)S(1)}, f32[1,4,256]{2,0,1:T(1,128)S(1)}, u32[]{:S(2)}, u32[]{:S(2)}) collective-permute-start(f32[1,4,256]{2,0,1:T(1,128)S(1)} %collective-permute-done.1), channel_id=1, source_target_pairs={{0,1},{1,2},{2,3},{3,4},{4,5},{5,6},{6,7},{7,8},{8,9},{9,10},{10,1... | collective-permute-start | bytes 12296 | tf_op jit(solution)/shard_map/ppermute | solution.py:16
  69.7 5.7 %collective-permute-start.3 = (f32[1,4,256]{2,0,1:T(1,128)S(1)}, f32[1,4,256]{2,0,1:T(1,128)S(1)}, u32[]{:S(2)}, u32[]{:S(2)}) collective-permute-start(f32[1,4,256]{2,0,1:T(1,128)S(1)} %collective-permute-done.2), channel_id=1, source_target_pairs={{0,1},{1,2},{2,3},{3,4},{4,5},{5,6},{6,7},{7,8},{8,9},{9,10},{10,1... | collective-permute-start | bytes 12296 | tf_op jit(solution)/shard_map/ppermute | solution.py:16
  75.5 5.7 %collective-permute-start.4 = (f32[1,4,256]{2,0,1:T(1,128)S(1)}, f32[1,4,256]{2,0,1:T(1,128)S(1)}, u32[]{:S(2)}, u32[]{:S(2)}) collective-permute-start(f32[1,4,256]{2,0,1:T(1,128)S(1)} %collective-permute-done.3), channel_id=1, source_target_pairs={{0,1},{1,2},{2,3},{3,4},{4,5},{5,6},{6,7},{7,8},{8,9},{9,10},{10,1... | collective-permute-start | bytes 12296 | tf_op jit(solution)/shard_map/ppermute | solution.py:16
  81.2 5.7 %collective-permute-start.5 = (f32[1,4,256]{2,0,1:T(1,128)S(1)}, f32[1,4,256]{2,0,1:T(1,128)S(1)}, u32[]{:S(2)}, u32[]{:S(2)}) collective-permute-start(f32[1,4,256]{2,0,1:T(1,128)S(1)} %collective-permute-done.4), channel_id=1, source_target_pairs={{0,1},{1,2},{2,3},{3,4},{4,5},{5,6},{6,7},{7,8},{8,9},{9,10},{10,1... | collective-permute-start | bytes 12296 | tf_op jit(solution)/shard_map/ppermute | solution.py:16
  86.9 5.7 %collective-permute-start.6 = (f32[1,4,256]{2,0,1:T(1,128)S(1)}, f32[1,4,256]{2,0,1:T(1,128)S(1)}, u32[]{:S(2)}, u32[]{:S(2)}) collective-permute-start(f32[1,4,256]{2,0,1:T(1,128)S(1)} %collective-permute-done.5), channel_id=1, source_target_pairs={{0,1},{1,2},{2,3},{3,4},{4,5},{5,6},{6,7},{7,8},{8,9},{9,10},{10,1... | collective-permute-start | bytes 12296 | tf_op jit(solution)/shard_map/ppermute | solution.py:16
  92.7 5.7 %collective-permute-start.7 = (f32[1,4,256]{2,0,1:T(1,128)S(1)}, f32[1,4,256]{2,0,1:T(1,128)S(1)}, u32[]{:S(2)}, u32[]{:S(2)}) collective-permute-start(f32[1,4,256]{2,0,1:T(1,128)S(1)} %collective-permute-done.6), channel_id=1, source_target_pairs={{0,1},{1,2},{2,3},{3,4},{4,5},{5,6},{6,7},{7,8},{8,9},{9,10},{10,1... | collective-permute-start | bytes 12296 | tf_op jit(solution)/shard_map/ppermute | solution.py:16
  98.4 5.7 %collective-permute-start.8 = (f32[1,4,256]{2,0,1:T(1,128)S(1)}, f32[1,4,256]{2,0,1:T(1,128)S(1)}, u32[]{:S(2)}, u32[]{:S(2)}) collective-permute-start(f32[1,4,256]{2,0,1:T(1,128)S(1)} %collective-permute-done.7), channel_id=1, source_target_pairs={{0,1},{1,2},{2,3},{3,4},{4,5},{5,6},{6,7},{7,8},{8,9},{9,10},{10,1... | collective-permute-start | bytes 12296 | tf_op jit(solution)/shard_map/ppermute | solution.py:16
  104.1 5.7 %collective-permute-start.9 = (f32[1,4,256]{2,0,1:T(1,128)S(1)}, f32[1,4,256]{2,0,1:T(1,128)S(1)}, u32[]{:S(2)}, u32[]{:S(2)}) collective-permute-start(f32[1,4,256]{2,0,1:T(1,128)S(1)} %collective-permute-done.8), channel_id=1, source_target_pairs={{0,1},{1,2},{2,3},{3,4},{4,5},{5,6},{6,7},{7,8},{8,9},{9,10},{10,1... | collective-permute-start | bytes 12296 | tf_op jit(solution)/shard_map/ppermute | solution.py:16
  109.8 5.7 %collective-permute-start.10 = (f32[1,4,256]{2,0,1:T(1,128)S(1)}, f32[1,4,256]{2,0,1:T(1,128)S(1)}, u32[]{:S(2)}, u32[]{:S(2)}) collective-permute-start(f32[1,4,256]{2,0,1:T(1,128)S(1)} %collective-permute-done.9), channel_id=1, source_target_pairs={{0,1},{1,2},{2,3},{3,4},{4,5},{5,6},{6,7},{7,8},{8,9},{9,10},{10,1... | collective-permute-start | bytes 12296 | tf_op jit(solution)/shard_map/ppermute | solution.py:16
  115.6 5.7 %collective-permute-start.11 = (f32[1,4,256]{2,0,1:T(1,128)S(1)}, f32[1,4,256]{2,0,1:T(1,128)S(1)}, u32[]{:S(2)}, u32[]{:S(2)}) collective-permute-start(f32[1,4,256]{2,0,1:T(1,128)S(1)} %collective-permute-done.10), channel_id=1, source_target_pairs={{0,1},{1,2},{2,3},{3,4},{4,5},{5,6},{6,7},{7,8},{8,9},{9,10},{10,1... | collective-permute-start | bytes 12296 | tf_op jit(solution)/shard_map/ppermute | solution.py:16
  121.3 5.7 %collective-permute-start.12 = (f32[1,4,256]{2,0,1:T(1,128)S(1)}, f32[1,4,256]{2,0,1:T(1,128)S(1)}, u32[]{:S(2)}, u32[]{:S(2)}) collective-permute-start(f32[1,4,256]{2,0,1:T(1,128)S(1)} %collective-permute-done.11), channel_id=1, source_target_pairs={{0,1},{1,2},{2,3},{3,4},{4,5},{5,6},{6,7},{7,8},{8,9},{9,10},{10,1... | collective-permute-start | bytes 12296 | tf_op jit(solution)/shard_map/ppermute | solution.py:16
  127.0 5.7 %collective-permute-start.13 = (f32[1,4,256]{2,0,1:T(1,128)S(1)}, f32[1,4,256]{2,0,1:T(1,128)S(1)}, u32[]{:S(2)}, u32[]{:S(2)}) collective-permute-start(f32[1,4,256]{2,0,1:T(1,128)S(1)} %collective-permute-done.12), channel_id=1, source_target_pairs={{0,1},{1,2},{2,3},{3,4},{4,5},{5,6},{6,7},{7,8},{8,9},{9,10},{10,1... | collective-permute-start | bytes 12296 | tf_op jit(solution)/shard_map/ppermute | solution.py:16
  132.8 5.7 %collective-permute-start.14 = (f32[1,4,256]{2,0,1:T(1,128)S(1)}, f32[1,4,256]{2,0,1:T(1,128)S(1)}, u32[]{:S(2)}, u32[]{:S(2)}) collective-permute-start(f32[1,4,256]{2,0,1:T(1,128)S(1)} %collective-permute-done.13), channel_id=1, source_target_pairs={{0,1},{1,2},{2,3},{3,4},{4,5},{5,6},{6,7},{7,8},{8,9},{9,10},{10,1... | collective-permute-start | bytes 12296 | tf_op jit(solution)/shard_map/ppermute | solution.py:16
  146.8 5.8 %collective-permute-start.15 = (f32[1,4,256]{2,0,1:T(1,128)S(1)}, f32[1,4,256]{2,0,1:T(1,128)S(1)}, u32[]{:S(2)}, u32[]{:S(2)}) collective-permute-start(f32[1,4,256]{2,0,1:T(1,128)S(1)} %slice_bitcast_fusion.23), channel_id=1, source_target_pairs={{0,1},{1,2},{2,3},{3,4},{4,5},{5,6},{6,7},{7,8},{8,9},{9,10},{10,1... | collective-permute-start | bytes 12296 | tf_op jit(solution)/shard_map/ppermute | solution.py:16
  152.6 5.7 %collective-permute-start.16 = (f32[1,4,256]{2,0,1:T(1,128)S(1)}, f32[1,4,256]{2,0,1:T(1,128)S(1)}, u32[]{:S(2)}, u32[]{:S(2)}) collective-permute-start(f32[1,4,256]{2,0,1:T(1,128)S(1)} %collective-permute-done.15), channel_id=1, source_target_pairs={{0,1},{1,2},{2,3},{3,4},{4,5},{5,6},{6,7},{7,8},{8,9},{9,10},{10,1... | collective-permute-start | bytes 12296 | tf_op jit(solution)/shard_map/ppermute | solution.py:16
  158.3 5.7 %collective-permute-start.17 = (f32[1,4,256]{2,0,1:T(1,128)S(1)}, f32[1,4,256]{2,0,1:T(1,128)S(1)}, u32[]{:S(2)}, u32[]{:S(2)}) collective-permute-start(f32[1,4,256]{2,0,1:T(1,128)S(1)} %collective-permute-done.16), channel_id=1, source_target_pairs={{0,1},{1,2},{2,3},{3,4},{4,5},{5,6},{6,7},{7,8},{8,9},{9,10},{10,1... | collective-permute-start | bytes 12296 | tf_op jit(solution)/shard_map/ppermute | solution.py:16
  164.0 5.7 %collective-permute-start.18 = (f32[1,4,256]{2,0,1:T(1,128)S(1)}, f32[1,4,256]{2,0,1:T(1,128)S(1)}, u32[]{:S(2)}, u32[]{:S(2)}) collective-permute-start(f32[1,4,256]{2,0,1:T(1,128)S(1)} %collective-permute-done.17), channel_id=1, source_target_pairs={{0,1},{1,2},{2,3},{3,4},{4,5},{5,6},{6,7},{7,8},{8,9},{9,10},{10,1... | collective-permute-start | bytes 12296 | tf_op jit(solution)/shard_map/ppermute | solution.py:16
  169.8 5.7 %collective-permute-start.19 = (f32[1,4,256]{2,0,1:T(1,128)S(1)}, f32[1,4,256]{2,0,1:T(1,128)S(1)}, u32[]{:S(2)}, u32[]{:S(2)}) collective-permute-start(f32[1,4,256]{2,0,1:T(1,128)S(1)} %collective-permute-done.18), channel_id=1, source_target_pairs={{0,1},{1,2},{2,3},{3,4},{4,5},{5,6},{6,7},{7,8},{8,9},{9,10},{10,1... | collective-permute-start | bytes 12296 | tf_op jit(solution)/shard_map/ppermute | solution.py:16
  175.5 5.7 %collective-permute-start.20 = (f32[1,4,256]{2,0,1:T(1,128)S(1)}, f32[1,4,256]{2,0,1:T(1,128)S(1)}, u32[]{:S(2)}, u32[]{:S(2)}) collective-permute-start(f32[1,4,256]{2,0,1:T(1,128)S(1)} %collective-permute-done.19), channel_id=1, source_target_pairs={{0,1},{1,2},{2,3},{3,4},{4,5},{5,6},{6,7},{7,8},{8,9},{9,10},{10,1... | collective-permute-start | bytes 12296 | tf_op jit(solution)/shard_map/ppermute | solution.py:16
  181.2 5.7 %collective-permute-start.21 = (f32[1,4,256]{2,0,1:T(1,128)S(1)}, f32[1,4,256]{2,0,1:T(1,128)S(1)}, u32[]{:S(2)}, u32[]{:S(2)}) collective-permute-start(f32[1,4,256]{2,0,1:T(1,128)S(1)} %collective-permute-done.20), channel_id=1, source_target_pairs={{0,1},{1,2},{2,3},{3,4},{4,5},{5,6},{6,7},{7,8},{8,9},{9,10},{10,1... | collective-permute-start | bytes 12296 | tf_op jit(solution)/shard_map/ppermute | solution.py:16
  187.0 5.7 %collective-permute-start.22 = (f32[1,4,256]{2,0,1:T(1,128)S(1)}, f32[1,4,256]{2,0,1:T(1,128)S(1)}, u32[]{:S(2)}, u32[]{:S(2)}) collective-permute-start(f32[1,4,256]{2,0,1:T(1,128)S(1)} %collective-permute-done.21), channel_id=1, source_target_pairs={{0,1},{1,2},{2,3},{3,4},{4,5},{5,6},{6,7},{7,8},{8,9},{9,10},{10,1... | collective-permute-start | bytes 12296 | tf_op jit(solution)/shard_map/ppermute | solution.py:16
  192.7 5.7 %collective-permute-start.23 = (f32[1,4,256]{2,0,1:T(1,128)S(1)}, f32[1,4,256]{2,0,1:T(1,128)S(1)}, u32[]{:S(2)}, u32[]{:S(2)}) collective-permute-start(f32[1,4,256]{2,0,1:T(1,128)S(1)} %collective-permute-done.22), channel_id=1, source_target_pairs={{0,1},{1,2},{2,3},{3,4},{4,5},{5,6},{6,7},{7,8},{8,9},{9,10},{10,1... | collective-permute-start | bytes 12296 | tf_op jit(solution)/shard_map/ppermute | solution.py:16
  198.4 5.7 %collective-permute-start.24 = (f32[1,4,256]{2,0,1:T(1,128)S(1)}, f32[1,4,256]{2,0,1:T(1,128)S(1)}, u32[]{:S(2)}, u32[]{:S(2)}) collective-permute-start(f32[1,4,256]{2,0,1:T(1,128)S(1)} %collective-permute-done.23), channel_id=1, source_target_pairs={{0,1},{1,2},{2,3},{3,4},{4,5},{5,6},{6,7},{7,8},{8,9},{9,10},{10,1... | collective-permute-start | bytes 12296 | tf_op jit(solution)/shard_map/ppermute | solution.py:16
  204.2 5.7 %collective-permute-start.25 = (f32[1,4,256]{2,0,1:T(1,128)S(1)}, f32[1,4,256]{2,0,1:T(1,128)S(1)}, u32[]{:S(2)}, u32[]{:S(2)}) collective-permute-start(f32[1,4,256]{2,0,1:T(1,128)S(1)} %collective-permute-done.24), channel_id=1, source_target_pairs={{0,1},{1,2},{2,3},{3,4},{4,5},{5,6},{6,7},{7,8},{8,9},{9,10},{10,1... | collective-permute-start | bytes 12296 | tf_op jit(solution)/shard_map/ppermute | solution.py:16
  209.9 5.7 %collective-permute-start.26 = (f32[1,4,256]{2,0,1:T(1,128)S(1)}, f32[1,4,256]{2,0,1:T(1,128)S(1)}, u32[]{:S(2)}, u32[]{:S(2)}) collective-permute-start(f32[1,4,256]{2,0,1:T(1,128)S(1)} %collective-permute-done.25), channel_id=1, source_target_pairs={{0,1},{1,2},{2,3},{3,4},{4,5},{5,6},{6,7},{7,8},{8,9},{9,10},{10,1... | collective-permute-start | bytes 12296 | tf_op jit(solution)/shard_map/ppermute | solution.py:16
  215.6 5.7 %collective-permute-start.27 = (f32[1,4,256]{2,0,1:T(1,128)S(1)}, f32[1,4,256]{2,0,1:T(1,128)S(1)}, u32[]{:S(2)}, u32[]{:S(2)}) collective-permute-start(f32[1,4,256]{2,0,1:T(1,128)S(1)} %collective-permute-done.26), channel_id=1, source_target_pairs={{0,1},{1,2},{2,3},{3,4},{4,5},{5,6},{6,7},{7,8},{8,9},{9,10},{10,1... | collective-permute-start | bytes 12296 | tf_op jit(solution)/shard_map/ppermute | solution.py:16
  221.3 5.7 %collective-permute-start.28 = (f32[1,4,256]{2,0,1:T(1,128)S(1)}, f32[1,4,256]{2,0,1:T(1,128)S(1)}, u32[]{:S(2)}, u32[]{:S(2)}) collective-permute-start(f32[1,4,256]{2,0,1:T(1,128)S(1)} %collective-permute-done.27), channel_id=1, source_target_pairs={{0,1},{1,2},{2,3},{3,4},{4,5},{5,6},{6,7},{7,8},{8,9},{9,10},{10,1... | collective-permute-start | bytes 12296 | tf_op jit(solution)/shard_map/ppermute | solution.py:16
  227.1 5.7 %collective-permute-start.29 = (f32[1,4,256]{2,0,1:T(1,128)S(1)}, f32[1,4,256]{2,0,1:T(1,128)S(1)}, u32[]{:S(2)}, u32[]{:S(2)}) collective-permute-start(f32[1,4,256]{2,0,1:T(1,128)S(1)} %collective-permute-done.28), channel_id=1, source_target_pairs={{0,1},{1,2},{2,3},{3,4},{4,5},{5,6},{6,7},{7,8},{8,9},{9,10},{10,1... | collective-permute-start | bytes 12296 | tf_op jit(solution)/shard_map/ppermute | solution.py:16
  250.4 34.5 %collective-permute-start.30 = (f32[1,4,256]{2,0,1:T(1,128)S(1)}, f32[1,4,256]{2,0,1:T(1,128)S(1)}, u32[]{:S(2)}, u32[]{:S(2)}) collective-permute-start(f32[1,4,256]{2,0,1:T(1,128)S(1)} %slice_bitcast_fusion.19), channel_id=1, source_target_pairs={{0,1},{1,2},{2,3},{3,4},{4,5},{5,6},{6,7},{7,8},{8,9},{9,10},{10,1... | collective-permute-start | bytes 12296 | tf_op jit(solution)/shard_map/ppermute | solution.py:16
  284.9 5.7 %collective-permute-start.31 = (f32[1,4,256]{2,0,1:T(1,128)S(1)}, f32[1,4,256]{2,0,1:T(1,128)S(1)}, u32[]{:S(2)}, u32[]{:S(2)}) collective-permute-start(f32[1,4,256]{2,0,1:T(1,128)S(1)} %collective-permute-done.30), channel_id=1, source_target_pairs={{0,1},{1,2},{2,3},{3,4},{4,5},{5,6},{6,7},{7,8},{8,9},{9,10},{10,1... | collective-permute-start | bytes 12296 | tf_op jit(solution)/shard_map/ppermute | solution.py:16
  290.6 5.7 %collective-permute-start.32 = (f32[1,4,256]{2,0,1:T(1,128)S(1)}, f32[1,4,256]{2,0,1:T(1,128)S(1)}, u32[]{:S(2)}, u32[]{:S(2)}) collective-permute-start(f32[1,4,256]{2,0,1:T(1,128)S(1)} %collective-permute-done.31), channel_id=1, source_target_pairs={{0,1},{1,2},{2,3},{3,4},{4,5},{5,6},{6,7},{7,8},{8,9},{9,10},{10,1... | collective-permute-start | bytes 12296 | tf_op jit(solution)/shard_map/ppermute | solution.py:16
  296.4 5.7 %collective-permute-start.33 = (f32[1,4,256]{2,0,1:T(1,128)S(1)}, f32[1,4,256]{2,0,1:T(1,128)S(1)}, u32[]{:S(2)}, u32[]{:S(2)}) collective-permute-start(f32[1,4,256]{2,0,1:T(1,128)S(1)} %collective-permute-done.32), channel_id=1, source_target_pairs={{0,1},{1,2},{2,3},{3,4},{4,5},{5,6},{6,7},{7,8},{8,9},{9,10},{10,1... | collective-permute-start | bytes 12296 | tf_op jit(solution)/shard_map/ppermute | solution.py:16
  302.1 5.7 %collective-permute-start.34 = (f32[1,4,256]{2,0,1:T(1,128)S(1)}, f32[1,4,256]{2,0,1:T(1,128)S(1)}, u32[]{:S(2)}, u32[]{:S(2)}) collective-permute-start(f32[1,4,256]{2,0,1:T(1,128)S(1)} %collective-permute-done.33), channel_id=1, source_target_pairs={{0,1},{1,2},{2,3},{3,4},{4,5},{5,6},{6,7},{7,8},{8,9},{9,10},{10,1... | collective-permute-start | bytes 12296 | tf_op jit(solution)/shard_map/ppermute | solution.py:16
  307.8 5.7 %collective-permute-start.35 = (f32[1,4,256]{2,0,1:T(1,128)S(1)}, f32[1,4,256]{2,0,1:T(1,128)S(1)}, u32[]{:S(2)}, u32[]{:S(2)}) collective-permute-start(f32[1,4,256]{2,0,1:T(1,128)S(1)} %collective-permute-done.34), channel_id=1, source_target_pairs={{0,1},{1,2},{2,3},{3,4},{4,5},{5,6},{6,7},{7,8},{8,9},{9,10},{10,1... | collective-permute-start | bytes 12296 | tf_op jit(solution)/shard_map/ppermute | solution.py:16
  313.6 5.7 %collective-permute-start.36 = (f32[1,4,256]{2,0,1:T(1,128)S(1)}, f32[1,4,256]{2,0,1:T(1,128)S(1)}, u32[]{:S(2)}, u32[]{:S(2)}) collective-permute-start(f32[1,4,256]{2,0,1:T(1,128)S(1)} %collective-permute-done.35), channel_id=1, source_target_pairs={{0,1},{1,2},{2,3},{3,4},{4,5},{5,6},{6,7},{7,8},{8,9},{9,10},{10,1... | collective-permute-start | bytes 12296 | tf_op jit(solution)/shard_map/ppermute | solution.py:16
  319.3 5.7 %collective-permute-start.37 = (f32[1,4,256]{2,0,1:T(1,128)S(1)}, f32[1,4,256]{2,0,1:T(1,128)S(1)}, u32[]{:S(2)}, u32[]{:S(2)}) collective-permute-start(f32[1,4,256]{2,0,1:T(1,128)S(1)} %collective-permute-done.36), channel_id=1, source_target_pairs={{0,1},{1,2},{2,3},{3,4},{4,5},{5,6},{6,7},{7,8},{8,9},{9,10},{10,1... | collective-permute-start | bytes 12296 | tf_op jit(solution)/shard_map/ppermute | solution.py:16
  325.0 5.7 %collective-permute-start.38 = (f32[1,4,256]{2,0,1:T(1,128)S(1)}, f32[1,4,256]{2,0,1:T(1,128)S(1)}, u32[]{:S(2)}, u32[]{:S(2)}) collective-permute-start(f32[1,4,256]{2,0,1:T(1,128)S(1)} %collective-permute-done.37), channel_id=1, source_target_pairs={{0,1},{1,2},{2,3},{3,4},{4,5},{5,6},{6,7},{7,8},{8,9},{9,10},{10,1... | collective-permute-start | bytes 12296 | tf_op jit(solution)/shard_map/ppermute | solution.py:16
  330.8 5.7 %collective-permute-start.39 = (f32[1,4,256]{2,0,1:T(1,128)S(1)}, f32[1,4,256]{2,0,1:T(1,128)S(1)}, u32[]{:S(2)}, u32[]{:S(2)}) collective-permute-start(f32[1,4,256]{2,0,1:T(1,128)S(1)} %collective-permute-done.38), channel_id=1, source_target_pairs={{0,1},{1,2},{2,3},{3,4},{4,5},{5,6},{6,7},{7,8},{8,9},{9,10},{10,1... | collective-permute-start | bytes 12296 | tf_op jit(solution)/shard_map/ppermute | solution.py:16
  336.5 5.7 %collective-permute-start.40 = (f32[1,4,256]{2,0,1:T(1,128)S(1)}, f32[1,4,256]{2,0,1:T(1,128)S(1)}, u32[]{:S(2)}, u32[]{:S(2)}) collective-permute-start(f32[1,4,256]{2,0,1:T(1,128)S(1)} %collective-permute-done.39), channel_id=1, source_target_pairs={{0,1},{1,2},{2,3},{3,4},{4,5},{5,6},{6,7},{7,8},{8,9},{9,10},{10,1... | collective-permute-start | bytes 12296 | tf_op jit(solution)/shard_map/ppermute | solution.py:16
  342.2 5.7 %collective-permute-start.41 = (f32[1,4,256]{2,0,1:T(1,128)S(1)}, f32[1,4,256]{2,0,1:T(1,128)S(1)}, u32[]{:S(2)}, u32[]{:S(2)}) collective-permute-start(f32[1,4,256]{2,0,1:T(1,128)S(1)} %collective-permute-done.40), channel_id=1, source_target_pairs={{0,1},{1,2},{2,3},{3,4},{4,5},{5,6},{6,7},{7,8},{8,9},{9,10},{10,1... | collective-permute-start | bytes 12296 | tf_op jit(solution)/shard_map/ppermute | solution.py:16
  347.9 5.7 %collective-permute-start.42 = (f32[1,4,256]{2,0,1:T(1,128)S(1)}, f32[1,4,256]{2,0,1:T(1,128)S(1)}, u32[]{:S(2)}, u32[]{:S(2)}) collective-permute-start(f32[1,4,256]{2,0,1:T(1,128)S(1)} %collective-permute-done.41), channel_id=1, source_target_pairs={{0,1},{1,2},{2,3},{3,4},{4,5},{5,6},{6,7},{7,8},{8,9},{9,10},{10,1... | collective-permute-start | bytes 12296 | tf_op jit(solution)/shard_map/ppermute | solution.py:16
  353.7 5.7 %collective-permute-start.43 = (f32[1,4,256]{2,0,1:T(1,128)S(1)}, f32[1,4,256]{2,0,1:T(1,128)S(1)}, u32[]{:S(2)}, u32[]{:S(2)}) collective-permute-start(f32[1,4,256]{2,0,1:T(1,128)S(1)} %collective-permute-done.42), channel_id=1, source_target_pairs={{0,1},{1,2},{2,3},{3,4},{4,5},{5,6},{6,7},{7,8},{8,9},{9,10},{10,1... | collective-permute-start | bytes 12296 | tf_op jit(solution)/shard_map/ppermute | solution.py:16
  359.4 5.7 %collective-permute-start.44 = (f32[1,4,256]{2,0,1:T(1,128)S(1)}, f32[1,4,256]{2,0,1:T(1,128)S(1)}, u32[]{:S(2)}, u32[]{:S(2)}) collective-permute-start(f32[1,4,256]{2,0,1:T(1,128)S(1)} %collective-permute-done.43), channel_id=1, source_target_pairs={{0,1},{1,2},{2,3},{3,4},{4,5},{5,6},{6,7},{7,8},{8,9},{9,10},{10,1... | collective-permute-start | bytes 12296 | tf_op jit(solution)/shard_map/ppermute | solution.py:16
  384.1 5.8 %collective-permute-start.45 = (f32[1,4,256]{2,0,1:T(1,128)S(1)}, f32[1,4,256]{2,0,1:T(1,128)S(1)}, u32[]{:S(2)}, u32[]{:S(2)}) collective-permute-start(f32[1,4,256]{2,0,1:T(1,128)S(1)} %slice_bitcast_fusion.15), channel_id=1, source_target_pairs={{0,1},{1,2},{2,3},{3,4},{4,5},{5,6},{6,7},{7,8},{8,9},{9,10},{10,1... | collective-permute-start | bytes 12296 | tf_op jit(solution)/shard_map/ppermute | solution.py:16
  389.9 5.7 %collective-permute-start.46 = (f32[1,4,256]{2,0,1:T(1,128)S(1)}, f32[1,4,256]{2,0,1:T(1,128)S(1)}, u32[]{:S(2)}, u32[]{:S(2)}) collective-permute-start(f32[1,4,256]{2,0,1:T(1,128)S(1)} %collective-permute-done.45), channel_id=1, source_target_pairs={{0,1},{1,2},{2,3},{3,4},{4,5},{5,6},{6,7},{7,8},{8,9},{9,10},{10,1... | collective-permute-start | bytes 12296 | tf_op jit(solution)/shard_map/ppermute | solution.py:16
  395.6 5.7 %collective-permute-start.47 = (f32[1,4,256]{2,0,1:T(1,128)S(1)}, f32[1,4,256]{2,0,1:T(1,128)S(1)}, u32[]{:S(2)}, u32[]{:S(2)}) collective-permute-start(f32[1,4,256]{2,0,1:T(1,128)S(1)} %collective-permute-done.46), channel_id=1, source_target_pairs={{0,1},{1,2},{2,3},{3,4},{4,5},{5,6},{6,7},{7,8},{8,9},{9,10},{10,1... | collective-permute-start | bytes 12296 | tf_op jit(solution)/shard_map/ppermute | solution.py:16
  401.3 5.7 %collective-permute-start.48 = (f32[1,4,256]{2,0,1:T(1,128)S(1)}, f32[1,4,256]{2,0,1:T(1,128)S(1)}, u32[]{:S(2)}, u32[]{:S(2)}) collective-permute-start(f32[1,4,256]{2,0,1:T(1,128)S(1)} %collective-permute-done.47), channel_id=1, source_target_pairs={{0,1},{1,2},{2,3},{3,4},{4,5},{5,6},{6,7},{7,8},{8,9},{9,10},{10,1... | collective-permute-start | bytes 12296 | tf_op jit(solution)/shard_map/ppermute | solution.py:16
  407.1 5.7 %collective-permute-start.49 = (f32[1,4,256]{2,0,1:T(1,128)S(1)}, f32[1,4,256]{2,0,1:T(1,128)S(1)}, u32[]{:S(2)}, u32[]{:S(2)}) collective-permute-start(f32[1,4,256]{2,0,1:T(1,128)S(1)} %collective-permute-done.48), channel_id=1, source_target_pairs={{0,1},{1,2},{2,3},{3,4},{4,5},{5,6},{6,7},{7,8},{8,9},{9,10},{10,1... | collective-permute-start | bytes 12296 | tf_op jit(solution)/shard_map/ppermute | solution.py:16
  412.8 5.7 %collective-permute-start.50 = (f32[1,4,256]{2,0,1:T(1,128)S(1)}, f32[1,4,256]{2,0,1:T(1,128)S(1)}, u32[]{:S(2)}, u32[]{:S(2)}) collective-permute-start(f32[1,4,256]{2,0,1:T(1,128)S(1)} %collective-permute-done.49), channel_id=1, source_target_pairs={{0,1},{1,2},{2,3},{3,4},{4,5},{5,6},{6,7},{7,8},{8,9},{9,10},{10,1... | collective-permute-start | bytes 12296 | tf_op jit(solution)/shard_map/ppermute | solution.py:16
  418.5 5.7 %collective-permute-start.51 = (f32[1,4,256]{2,0,1:T(1,128)S(1)}, f32[1,4,256]{2,0,1:T(1,128)S(1)}, u32[]{:S(2)}, u32[]{:S(2)}) collective-permute-start(f32[1,4,256]{2,0,1:T(1,128)S(1)} %collective-permute-done.50), channel_id=1, source_target_pairs={{0,1},{1,2},{2,3},{3,4},{4,5},{5,6},{6,7},{7,8},{8,9},{9,10},{10,1... | collective-permute-start | bytes 12296 | tf_op jit(solution)/shard_map/ppermute | solution.py:16
  424.2 5.7 %collective-permute-start.52 = (f32[1,4,256]{2,0,1:T(1,128)S(1)}, f32[1,4,256]{2,0,1:T(1,128)S(1)}, u32[]{:S(2)}, u32[]{:S(2)}) collective-permute-start(f32[1,4,256]{2,0,1:T(1,128)S(1)} %collective-permute-done.51), channel_id=1, source_target_pairs={{0,1},{1,2},{2,3},{3,4},{4,5},{5,6},{6,7},{7,8},{8,9},{9,10},{10,1... | collective-permute-start | bytes 12296 | tf_op jit(solution)/shard_map/ppermute | solution.py:16
  430.0 5.7 %collective-permute-start.53 = (f32[1,4,256]{2,0,1:T(1,128)S(1)}, f32[1,4,256]{2,0,1:T(1,128)S(1)}, u32[]{:S(2)}, u32[]{:S(2)}) collective-permute-start(f32[1,4,256]{2,0,1:T(1,128)S(1)} %collective-permute-done.52), channel_id=1, source_target_pairs={{0,1},{1,2},{2,3},{3,4},{4,5},{5,6},{6,7},{7,8},{8,9},{9,10},{10,1... | collective-permute-start | bytes 12296 | tf_op jit(solution)/shard_map/ppermute | solution.py:16
  435.7 5.7 %collective-permute-start.54 = (f32[1,4,256]{2,0,1:T(1,128)S(1)}, f32[1,4,256]{2,0,1:T(1,128)S(1)}, u32[]{:S(2)}, u32[]{:S(2)}) collective-permute-start(f32[1,4,256]{2,0,1:T(1,128)S(1)} %collective-permute-done.53), channel_id=1, source_target_pairs={{0,1},{1,2},{2,3},{3,4},{4,5},{5,6},{6,7},{7,8},{8,9},{9,10},{10,1... | collective-permute-start | bytes 12296 | tf_op jit(solution)/shard_map/ppermute | solution.py:16
  441.4 5.7 %collective-permute-start.55 = (f32[1,4,256]{2,0,1:T(1,128)S(1)}, f32[1,4,256]{2,0,1:T(1,128)S(1)}, u32[]{:S(2)}, u32[]{:S(2)}) collective-permute-start(f32[1,4,256]{2,0,1:T(1,128)S(1)} %collective-permute-done.54), channel_id=1, source_target_pairs={{0,1},{1,2},{2,3},{3,4},{4,5},{5,6},{6,7},{7,8},{8,9},{9,10},{10,1... | collective-permute-start | bytes 12296 | tf_op jit(solution)/shard_map/ppermute | solution.py:16
  447.2 5.7 %collective-permute-start.56 = (f32[1,4,256]{2,0,1:T(1,128)S(1)}, f32[1,4,256]{2,0,1:T(1,128)S(1)}, u32[]{:S(2)}, u32[]{:S(2)}) collective-permute-start(f32[1,4,256]{2,0,1:T(1,128)S(1)} %collective-permute-done.55), channel_id=1, source_target_pairs={{0,1},{1,2},{2,3},{3,4},{4,5},{5,6},{6,7},{7,8},{8,9},{9,10},{10,1... | collective-permute-start | bytes 12296 | tf_op jit(solution)/shard_map/ppermute | solution.py:16
  452.9 5.7 %collective-permute-start.57 = (f32[1,4,256]{2,0,1:T(1,128)S(1)}, f32[1,4,256]{2,0,1:T(1,128)S(1)}, u32[]{:S(2)}, u32[]{:S(2)}) collective-permute-start(f32[1,4,256]{2,0,1:T(1,128)S(1)} %collective-permute-done.56), channel_id=1, source_target_pairs={{0,1},{1,2},{2,3},{3,4},{4,5},{5,6},{6,7},{7,8},{8,9},{9,10},{10,1... | collective-permute-start | bytes 12296 | tf_op jit(solution)/shard_map/ppermute | solution.py:16
  458.6 5.7 %collective-permute-start.58 = (f32[1,4,256]{2,0,1:T(1,128)S(1)}, f32[1,4,256]{2,0,1:T(1,128)S(1)}, u32[]{:S(2)}, u32[]{:S(2)}) collective-permute-start(f32[1,4,256]{2,0,1:T(1,128)S(1)} %collective-permute-done.57), channel_id=1, source_target_pairs={{0,1},{1,2},{2,3},{3,4},{4,5},{5,6},{6,7},{7,8},{8,9},{9,10},{10,1... | collective-permute-start | bytes 12296 | tf_op jit(solution)/shard_map/ppermute | solution.py:16
  464.4 5.7 %collective-permute-start.59 = (f32[1,4,256]{2,0,1:T(1,128)S(1)}, f32[1,4,256]{2,0,1:T(1,128)S(1)}, u32[]{:S(2)}, u32[]{:S(2)}) collective-permute-start(f32[1,4,256]{2,0,1:T(1,128)S(1)} %collective-permute-done.58), channel_id=1, source_target_pairs={{0,1},{1,2},{2,3},{3,4},{4,5},{5,6},{6,7},{7,8},{8,9},{9,10},{10,1... | collective-permute-start | bytes 12296 | tf_op jit(solution)/shard_map/ppermute | solution.py:16
  (60 other events, 952.7 us)
